TPU v7x, 128 devices: a whole 4x4x4 slice. The times are simulated.
128 devices in a mesh: lon: 16 (over y_hi, z, core), lat: 8 (over y_lo, x).
Axes of the slice: x: 4, y: 4 (y_hi: 2, y_lo: 2; y = y_hi * 2 + y_lo), z: 4, core: 2. Of those that a mesh axis runs over, the one named last changes fastest.
Arguments:
- temp_before: float32 [25, 512, 2048], P(None, 'lat', 'lon'), may hold values from -8 to 8
- temp_now: float32 [25, 512, 2048], P(None, 'lat', 'lon'), may hold values from -8 to 8
- salt_before: float32 [25, 512, 2048], P(None, 'lat', 'lon'), may hold values from -4 to 4
- salt_now: float32 [25, 512, 2048], P(None, 'lat', 'lon'), may hold values from -4 to 4
- east_velocity: float32 [25, 512, 2048], P(None, 'lat', 'lon'), may hold values from -0.3 to 0.3, as said below
- north_velocity: float32 [25, 512, 2048], P(None, 'lat', 'lon'), may hold values from -0.3 to 0.3, as said below
- bottom_level: int32 [512, 2048], P('lat', 'lon'), may hold values from 0 to 25, as said below
Outputs:
- temp_out: float32 [25, 512, 2048], P(None, 'lat', 'lon')
- salt_out: float32 [25, 512, 2048], P(None, 'lat', 'lon')
- density_out: float32 [25, 512, 2048], P(None, 'lat', 'lon')
Inputs may be any that keep to these rules, and one draw needn't show every extreme that they name: `bottom_level`: cells at levels below a column's value are ocean, the others land; every column of row 0 is land. `east_velocity`: zero on every face that touches a land cell; the face east of column 2047 touches column 0. `north_velocity`: zero on every face that touches a land cell; on row 511 the north face of column i touches cell (511, 2047 - i) and carries the negative of that column's value.
All inputs are finite; a program needn't handle non-finite values.
Results may differ from a plain program's by a relative error of at most 0.00002.
Values sent between devices are 32-bit elements; how exact they have to be, the bound alone decides.
No kernel may reach another device: no remote copies, remote signals or barrier semaphores. Data moves between devices by JAX's collectives and lax.ppermute only.
A program may use at most 256 MiB of HBM per device.

v0:
```python
import jax
import jax.numpy as jnp
from jax import lax
from jax.sharding import PartitionSpec as P

asselin_gamma = 0.1
nu_base = 0.05
nu_conv = 0.2
level_depth = 160.0
alpha_zero = 0.1655
beta_zero = 0.76554
lambda_one = 0.05952
lambda_two = 0.00054914
mu_one = 0.0001497
mu_two = 1.109e-05
nu_cross = 0.0024341


def extended_2(value, sides, width, wrap):
    for axis, dim in sides:
        count, length = (lax.axis_size(axis), value.shape[dim])
        up = [(i, (i + 1) % count) for i in range(count if wrap else count - 1)]
        down = [(j, i) for i, j in up]
        last = lax.slice_in_dim(value, length - width, length, axis=dim)
        leading = lax.slice_in_dim(value, 0, width, axis=dim)
        before = lax.ppermute(last, axis, up)
        after = lax.ppermute(leading, axis, down)
        value = jnp.concatenate([before, value, after], axis=dim)
    return value


def passed_along(block, axis, distance):
    devices = range(lax.axis_size(axis))
    route = [((i - distance) % len(devices), i) for i in devices]
    return lax.ppermute(block, axis, route)


def from_behind(value, axis, by):
    count = lax.axis_size(axis)
    pairs = [(i, i + by) for i in range(count) if 0 <= i + by < count]
    return lax.ppermute(value, axis, pairs)


def density(temp, salt):
    depth = level_depth * (jnp.arange(temp.shape[0], dtype=jnp.float32) + 0.5)[:, None, None]
    warm = -alpha_zero * (1.0 + 0.5 * lambda_one * temp + mu_one * depth) * temp
    salty = beta_zero * (1.0 - 0.5 * lambda_two * salt - mu_two * depth) * salt
    return warm + salty - nu_cross * temp * salt


def divergence(extended, velocity, along):
    face_count = velocity.shape[along - 1]
    behind_far = lax.slice_in_dim(extended, 0, face_count, axis=along)
    behind = lax.slice_in_dim(extended, 1, face_count + 1, axis=along)
    ahead = lax.slice_in_dim(extended, 2, face_count + 2, axis=along)
    ahead_far = lax.slice_in_dim(extended, 3, face_count + 3, axis=along)
    flux = velocity * (7.0 * (behind + ahead) - (behind_far + ahead_far)) / 12.0
    flux = flux + jnp.abs(velocity) * (ahead_far - behind_far - 3.0 * (ahead - behind)) / 12.0
    return lax.slice_in_dim(flux, 1, face_count, axis=along) - lax.slice_in_dim(
        flux, 0, face_count - 1, axis=along
    )


def vertical_mixing(before, now, ocean_mask):
    density_now = density(now[0], now[1])
    density_jump = density_now[1:] - density_now[:-1]
    mixing_rates = (nu_base + nu_conv * jax.nn.sigmoid(-4.0 * density_jump)) * ocean_mask[1:]
    flux = mixing_rates * (before[:, 1:] - before[:, :-1])
    padding = jnp.zeros_like(flux[:, :1])
    return jnp.concatenate([flux, padding], 1) - jnp.concatenate([padding, flux], 1)


def advance(before, now, x_ext, y_ext, east_faces, north_faces, ocean_mask):
    change = -(divergence(x_ext, east_faces, 3) + divergence(y_ext, north_faces, 2))
    change = change + vertical_mixing(before, now, ocean_mask)
    after = (before + 2.0 * change) * ocean_mask
    filtered = now + asselin_gamma * (before - 2.0 * now + after)
    return (filtered, after)


def extend_tracers(now, at_fold, columns):
    x_ext = extended_2(now, (("lon", 3),), 2, True)
    y_part = extended_2(now, (("lat", 2),), 2, False)
    edge_rows = now[:, :, -2:, :]
    cycle_size = lax.axis_size("lon")
    pieces = edge_rows.reshape(
        edge_rows.shape[0], edge_rows.shape[1], 2, cycle_size, columns // cycle_size
    )
    spread = lax.all_to_all(pieces, "lon", split_axis=3, concat_axis=3, tiled=True)
    returned = lax.all_to_all(
        spread[:, :, :, ::-1, :], "lon", split_axis=3, concat_axis=3, tiled=True
    )
    partner_rows = returned.reshape(edge_rows.shape)
    mirror = partner_rows[:, :, ::-1, ::-1]
    north_rows = jnp.where(at_fold, mirror, y_part[:, :, -2:, :])
    y_ext = jnp.concatenate([y_part[:, :, :-2, :], north_rows], 2)
    return (x_ext, y_ext)


def on_device(
    temp_before, temp_now, salt_before, salt_now, east_velocity, north_velocity, bottom_level
):
    levels = temp_now.shape[0]
    columns = temp_now.shape[2]
    ocean_mask = (jnp.arange(levels, dtype=jnp.int32)[:, None, None] < bottom_level[None]).astype(
        jnp.float32
    )
    before = jnp.stack([temp_before, salt_before]) * ocean_mask
    now = jnp.stack([temp_now, salt_now]) * ocean_mask
    west_column = passed_along(east_velocity[:, :, -1:], "lon", 1)
    east_faces = jnp.concatenate([west_column, east_velocity], 2)
    south_row = from_behind(north_velocity[:, -1:, :], "lat", 1)
    north_faces = jnp.concatenate([south_row, north_velocity], 1)
    at_fold = lax.axis_index("lat") == lax.axis_size("lat") - 1
    for step_index in range(2):
        x_ext, y_ext = extend_tracers(now, at_fold, columns)
        before, now = advance(before, now, x_ext, y_ext, east_faces, north_faces, ocean_mask)
    final_density = density(now[0], now[1]) * ocean_mask
    return (now[0], now[1], final_density)


def solution(mesh):
    return jax.shard_map(
        on_device,
        mesh=mesh,
        in_specs=(
            P(None, "lat", "lon"),
            P(None, "lat", "lon"),
            P(None, "lat", "lon"),
            P(None, "lat", "lon"),
            P(None, "lat", "lon"),
            P(None, "lat", "lon"),
            P("lat", "lon"),
        ),
        out_specs=(P(None, "lat", "lon"), P(None, "lat", "lon"), P(None, "lat", "lon")),
        check_vma=False,
    )
```

profile of v0, /device:TPU:25, one launch (start us, length us, event | category | flops | bytes accessed | tf_op | source)
XLA Modules:
  0.0 146.9 jit_solution(7164898051214208194)
XLA Ops:
  0.7 1.6 %slice.173 = f32[25,1,128]{2,1,0:T(1,128)} slice(f32[25,64,128]{2,1,0:T(8,128)} %param.12), slice={[0:25], [63:64], [0:128]} | slice | bytes 25600 | tf_op jit(solution)/shard_map/slice | solution.py:112
  2.2 3.1 %collective-permute-start.3 = (f32[25,1,128]{2,1,0:T(1,128)}, f32[25,1,128]{2,1,0:T(1,128)}, u32[]{:S(2)}, u32[]{:S(2)}) collective-permute-start(f32[25,1,128]{2,1,0:T(1,128)} %slice.173), channel_id=1, source_target_pairs={{0,1},{1,2},{2,3},{3,4},{4,5},{5,6},{6,7},{8,9},{9,10},{10,11},{11... | collective-permute-start | bytes 38408 | tf_op jit(solution)/shard_map/ppermute | solution.py:41
  5.3 1.4 slice.164
  7.1 2.5 %collective-permute-start = (f32[25,64,1]{1,0,2:T(8,128)S(1)}, f32[25,64,1]{1,0,2:T(8,128)}, u32[]{:S(2)}, u32[]{:S(2)}) collective-permute-start(f32[25,64,1]{1,0,2:T(8,128)S(1)} %copy.111), channel_id=1, source_target_pairs={{120,0},{0,8},{8,16},{16,24},{24,32},{32,40},{40,48},{48,56},{56,6... | collective-permute-start | bytes 19208 | tf_op jit(solution)/shard_map/ppermute | solution.py:35
  9.8 3.6 %maximum_multiply_fusion.1 = (f32[2,25,64,128]{3,2,1,0:T(8,128)}, f32[2,25,64,128]{3,2,1,0:T(8,128)S(1)}) fusion(f32[1,25,64,128]{3,2,1,0:T(8,128)S(1)} %bitcast.54, f32[1,25,64,128]{3,2,1,0:T(8,128)} %bitcast.55, f32[25,64,128]{2,1,0:T(8,128)S(1)} %fusion.14, f32[1,25,64,128]{3,2,1,0:T(8,128)} %bitcast.56, f32[1,25,64,128]{3,2,1,0:T(8,128)} %bitcast.57), kind=kLoop, calls=%fused_computation.37 | loop fusion | flops 1638400 | bytes 7372800 | tf_op jit(solution)/shard_map/mul | solution.py:108
  14.1 4.3 %collective-permute-start.5 = (f32[2,25,2,128]{3,2,1,0:T(2,128)}, f32[2,25,2,128]{3,2,1,0:T(2,128)}, u32[]{:S(2)}, u32[]{:S(2)}) collective-permute-start(f32[2,25,2,128]{3,2,1,0:T(2,128)} %get-tuple-element.25), channel_id=1, source_target_pairs={{1,0},{2,1},{3,2},{4,3},{5,4},{6,5},{7,6},{9,8},{10,9},{11,10},{12... | collective-permute-start | bytes 153608 | tf_op jit(solution)/shard_map/ppermute | solution.py:27
  18.4 1.9 %collective-permute-start.4 = (f32[2,25,2,128]{3,2,1,0:T(2,128)}, f32[2,25,2,128]{3,2,1,0:T(2,128)}, u32[]{:S(2)}, u32[]{:S(2)}) collective-permute-start(f32[2,25,2,128]{3,2,1,0:T(2,128)} %get-tuple-element.26), channel_id=1, source_target_pairs={{0,1},{1,2},{2,3},{3,4},{4,5},{5,6},{6,7},{8,9},{9,10},{10,11},{11... | collective-permute-start | bytes 153608 | tf_op jit(solution)/shard_map/ppermute | solution.py:26
  20.3 0.9 copy.99
  21.3 0.9 reshape.71
  22.2 7.6 %all-to-all-start = ((f32[16,1,800]{2,1,0:T(1,128)}), f32[16,1,800]{2,1,0:T(1,128)S(1)}, u32[]{:S(2)}, u32[]{:S(2)}) async-start(f32[16,1,800]{2,1,0:T(1,128)} %reshape.71), calls=%async_computation | async-start | bytes 114688 | tf_op jit(solution)/shard_map/all_to_all | solution.py:89
  29.7 2.3 %fusion.34 = (f32[2,25,64,2]{3,2,1,0:T(8,128)}, f32[2,25,64,2]{3,2,1,0:T(8,128)}) fusion(f32[2,25,64,128]{3,2,1,0:T(8,128)S(1)} %get-tuple-element.30), kind=kLoop, calls=%fused_computation.83 | loop fusion | bytes 102400 | tf_op jit(solution)/shard_map/slice | solution.py:25
  32.0 2.0 %copy.95 = f32[2,25,64,2]{2,3,1,0:T(2,128)S(1)} copy(f32[2,25,64,2]{3,2,1,0:T(8,128)} %get-tuple-element.24) | data formatting | bytes 51200 | tf_op jit(solution)/shard_map/slice | solution.py:24
  34.0 1.5 %collective-permute-start.1 = (f32[2,25,64,2]{2,3,1,0:T(2,128)S(1)}, f32[2,25,64,2]{2,3,1,0:T(2,128)S(1)}, u32[]{:S(2)}, u32[]{:S(2)}) collective-permute-start(f32[2,25,64,2]{2,3,1,0:T(2,128)S(1)} %copy.95), channel_id=1, source_target_pairs={{0,8},{8,16},{16,24},{24,32},{32,40},{40,48},{48,56},{56,64},{64,7... | collective-permute-start | bytes 76808 | tf_op jit(solution)/shard_map/ppermute | solution.py:26
  36.2 1.2 copy-done.3
  37.3 1.5 fusion.13
  40.0 1.9 %copy.94 = f32[25,64,1]{2,1,0:T(8,128)} copy(f32[25,64,1]{1,0,2:T(8,128)} %collective-permute-done) | data formatting | bytes 12800 | tf_op jit(solution)/shard_map/ppermute | solution.py:35
  41.9 3.1 %pad_maximum_fusion.8 = (f32[25,64,129]{2,1,0:T(8,128)S(1)}, f32[25,64,129]{2,1,0:T(8,128)}) fusion(f32[25,64,128]{2,1,0:T(8,128)} %param.11, f32[25,64,1]{2,1,0:T(8,128)} %copy.94), kind=kLoop, calls=%fused_computation.38 | loop fusion | flops 412800 | bytes 2476800 | tf_op jit(solution)/shard_map/concatenate | solution.py:111
  45.1 2.1 %pad_maximum_fusion.9 = (f32[25,65,128]{2,1,0:T(8,128)}, f32[25,65,128]{2,1,0:T(8,128)}) fusion(f32[25,64,128]{2,1,0:T(8,128)S(1)} %copy-done.12, f32[25,1,128]{2,1,0:T(1,128)} %collective-permute-done.3), kind=kLoop, calls=%fused_computation.44 | loop fusion | flops 416000 | bytes 2496000 | tf_op jit(solution)/shard_map/concatenate | solution.py:113
  47.2 1.7 %copy.98 = f32[2,25,64,2]{3,2,1,0:T(8,128)} copy(f32[2,25,64,2]{2,3,1,0:T(2,128)S(1)} %collective-permute-done.2) | data formatting | bytes 51200 | tf_op jit(solution)/shard_map/ppermute | solution.py:27
  48.9 1.8 %copy.96 = f32[2,25,64,2]{3,2,1,0:T(8,128)} copy(f32[2,25,64,2]{2,3,1,0:T(2,128)S(1)} %collective-permute-done.1) | data formatting | bytes 51200 | tf_op jit(solution)/shard_map/ppermute | solution.py:26
  51.2 1.4 reduce
  52.6 1.1 reshape.72
  54.4 1.8 %reshape.73 = f32[16,1,800]{2,1,0:T(1,128)} reshape(f32[16,2,2,8,25]{4,3,2,1,0:T(8,128)} %reverse_bitcast_fusion.1) | data formatting | bytes 102400
  56.2 8.7 %all-to-all-start.1 = ((f32[16,1,800]{2,1,0:T(1,128)}), f32[16,1,800]{2,1,0:T(1,128)S(1)}, u32[]{:S(2)}, u32[]{:S(2)}) async-start(f32[16,1,800]{2,1,0:T(1,128)} %reshape.73), calls=%async_computation.1 | async-start | bytes 114688 | tf_op jit(solution)/shard_map/all_to_all | solution.py:90
  65.0 7.0 %add_multiply_fusion.1 = f32[2,25,64,129]{3,2,1,0:T(8,128)} fusion(f32[2,25,64,128]{3,2,1,0:T(8,128)S(1)} %get-tuple-element.30, f32[2,25,64,2]{3,2,1,0:T(8,128)} %copy.96, f32[2,25,64,2]{3,2,1,0:T(8,128)} %copy.98, f32[25,64,129]{2,1,0:T(8,128)} %get-tuple-element.22, f32[25,64,129]{2,1,0:T(8,128)S(1)} %get-tuple-element.21), kind=kLoop, calls=%fused_computation.9 | loop fusion | flops 6604800 | bytes 4992000 | tf_op jit(solution)/shard_map/add | solution.py:58
  73.5 0.8 broadcast_select_fusion.1
  74.4 2.6 %add_multiply_fusion.3 = f32[2,25,65,128]{3,2,1,0:T(8,128)S(1)} fusion(f32[2,25,64,128]{3,2,1,0:T(8,128)S(1)} %get-tuple-element.30, f32[2,25,2,128]{3,2,1,0:T(2,128)} %collective-permute-done.4, f32[2,25,2,128]{3,2,1,0:T(2,128)S(1)} %broadcast_select_fusion.1, f32[25,65,128]{2,1,0:T(8,128)} %get-tuple-element.28, f32[25,65,128]{2,1,0:T(8,128)S(1)} %copy-done.8), kind=kLoop, calls=%fused_computation.19 | loop fusion | flops 6656000 | bytes 5068800 | tf_op jit(solution)/shard_map/add | solution.py:58
  77.0 5.1 %multiply_add_fusion = (f32[2,25,64,128]{3,2,1,0:T(8,128)}, f32[2,25,64,128]{3,2,1,0:T(8,128)S(1)}) fusion(f32[2,25,64,128]{3,2,1,0:T(8,128)S(1)} %get-tuple-element.30, f32[2,25,64,128]{3,2,1,0:T(8,128)S(1)} %copy-done.4, f32[25,64,128]{2,1,0:T(8,128)S(1)} %copy-done.1, f32[2,24,64,128]{3,2,1,0:T(8,128)S(1)} %copy-done.10, ...), kind=kLoop, calls=%fused_computation.39 | loop fusion | flops 5734400 | bytes 15499264 | tf_op jit(solution)/shard_map/add | solution.py:77
  82.8 2.2 %collective-permute-start.8 = (f32[2,25,2,128]{3,2,1,0:T(2,128)}, f32[2,25,2,128]{3,2,1,0:T(2,128)}, u32[]{:S(2)}, u32[]{:S(2)}) collective-permute-start(f32[2,25,2,128]{3,2,1,0:T(2,128)} %get-tuple-element.20), channel_id=1, source_target_pairs={{0,1},{1,2},{2,3},{3,4},{4,5},{5,6},{6,7},{8,9},{9,10},{10,11},{11... | collective-permute-start | bytes 153608 | tf_op jit(solution)/shard_map/ppermute | solution.py:26
  85.0 0.9 copy.107
  86.4 2.3 %fusion.32 = (f32[2,25,64,2]{3,2,1,0:T(8,128)}, f32[2,25,64,2]{3,2,1,0:T(8,128)}) fusion(f32[2,25,64,128]{3,2,1,0:T(8,128)S(1)} %get-tuple-element.16), kind=kLoop, calls=%fused_computation.81 | loop fusion | bytes 102400 | tf_op jit(solution)/shard_map/slice | solution.py:25
  88.7 5.2 %collective-permute-start.9 = (f32[2,25,2,128]{3,2,1,0:T(2,128)}, f32[2,25,2,128]{3,2,1,0:T(2,128)}, u32[]{:S(2)}, u32[]{:S(2)}) collective-permute-start(f32[2,25,2,128]{3,2,1,0:T(2,128)} %get-tuple-element.19), channel_id=1, source_target_pairs={{1,0},{2,1},{3,2},{4,3},{5,4},{6,5},{7,6},{9,8},{10,9},{11,10},{12... | collective-permute-start | bytes 153608 | tf_op jit(solution)/shard_map/ppermute | solution.py:27
  94.6 1.8 %reshape.75 = f32[16,1,800]{2,1,0:T(1,128)} reshape(f32[16,2,2,8,25]{4,3,2,1,0:T(8,128)} %copy_bitcast_fusion.2) | data formatting | bytes 102400
  96.4 7.8 %all-to-all-start.2 = ((f32[16,1,800]{2,1,0:T(1,128)}), f32[16,1,800]{2,1,0:T(1,128)S(1)}, u32[]{:S(2)}, u32[]{:S(2)}) async-start(f32[16,1,800]{2,1,0:T(1,128)} %reshape.75), calls=%async_computation.2 | async-start | bytes 114688 | tf_op jit(solution)/shard_map/all_to_all | solution.py:89
  104.2 1.1 add_multiply_fusion.4
  105.3 2.1 %copy.105 = f32[2,25,64,2]{2,3,1,0:T(2,128)S(1)} copy(f32[2,25,64,2]{3,2,1,0:T(8,128)} %get-tuple-element.17) | data formatting | bytes 51200 | tf_op jit(solution)/shard_map/slice | solution.py:25
  107.4 2.0 %copy.103 = f32[2,25,64,2]{2,3,1,0:T(2,128)S(1)} copy(f32[2,25,64,2]{3,2,1,0:T(8,128)} %get-tuple-element.18) | data formatting | bytes 51200 | tf_op jit(solution)/shard_map/slice | solution.py:24
  109.4 1.5 %collective-permute-start.6 = (f32[2,25,64,2]{2,3,1,0:T(2,128)S(1)}, f32[2,25,64,2]{2,3,1,0:T(2,128)S(1)}, u32[]{:S(2)}, u32[]{:S(2)}) collective-permute-start(f32[2,25,64,2]{2,3,1,0:T(2,128)S(1)} %copy.103), channel_id=1, source_target_pairs={{0,8},{8,16},{16,24},{24,32},{32,40},{40,48},{48,56},{56,64},{64,7... | collective-permute-start | bytes 76808 | tf_op jit(solution)/shard_map/ppermute | solution.py:26
  110.9 3.6 %fusion.12 = f32[2,24,64,128]{3,2,1,0:T(8,128)} fusion(f32[2,25,64,128]{3,2,1,0:T(8,128)} %get-tuple-element.15, f32[24,64,128]{2,1,0:T(8,128)S(1)} %copy-done.11), kind=kLoop, calls=%fused_computation.41 | loop fusion | flops 786432 | bytes 5505024 | tf_op jit(solution)/shard_map/mul | solution.py:68
  114.7 1.7 %copy.106 = f32[2,25,64,2]{3,2,1,0:T(8,128)} copy(f32[2,25,64,2]{2,3,1,0:T(2,128)S(1)} %collective-permute-done.7) | data formatting | bytes 51200 | tf_op jit(solution)/shard_map/ppermute | solution.py:27
  116.5 1.8 %copy.104 = f32[2,25,64,2]{3,2,1,0:T(8,128)} copy(f32[2,25,64,2]{2,3,1,0:T(2,128)S(1)} %collective-permute-done.6) | data formatting | bytes 51200 | tf_op jit(solution)/shard_map/ppermute | solution.py:26
  119.3 0.9 reshape.77
  120.2 9.1 %all-to-all-start.3 = ((f32[16,1,800]{2,1,0:T(1,128)}), f32[16,1,800]{2,1,0:T(1,128)S(1)}, u32[]{:S(2)}, u32[]{:S(2)}) async-start(f32[16,1,800]{2,1,0:T(1,128)} %reshape.77), calls=%async_computation.3 | async-start | bytes 114688 | tf_op jit(solution)/shard_map/all_to_all | solution.py:90
  129.2 7.2 %add_multiply_fusion = f32[2,25,64,129]{3,2,1,0:T(8,128)} fusion(f32[2,25,64,128]{3,2,1,0:T(8,128)S(1)} %get-tuple-element.16, f32[2,25,64,2]{3,2,1,0:T(8,128)} %copy.104, f32[2,25,64,2]{3,2,1,0:T(8,128)} %copy.106, f32[25,64,129]{2,1,0:T(8,128)} %get-tuple-element.22, f32[25,64,129]{2,1,0:T(8,128)} %copy-done.6), kind=kLoop, calls=%fused_computation.8 | loop fusion | flops 6604800 | bytes 4992000 | tf_op jit(solution)/shard_map/add | solution.py:58
  137.9 0.8 broadcast_select_fusion
  138.8 2.7 %add_multiply_fusion.2 = f32[2,25,65,128]{3,2,1,0:T(8,128)S(1)} fusion(f32[2,25,64,128]{3,2,1,0:T(8,128)S(1)} %get-tuple-element.16, f32[2,25,2,128]{3,2,1,0:T(2,128)} %collective-permute-done.8, f32[2,25,2,128]{3,2,1,0:T(2,128)S(1)} %broadcast_select_fusion, f32[25,65,128]{2,1,0:T(8,128)} %get-tuple-element.28, f32[25,65,128]{2,1,0:T(8,128)} %get-tuple-element.27), kind=kLoop, calls=%fused_computation.18 | loop fusion | flops 6656000 | bytes 5068800 | tf_op jit(solution)/shard_map/add | solution.py:58
  141.8 3.2 %fusion.5 = f32[2,25,64,128]{3,2,1,0:T(8,128)S(1)} fusion(f32[2,25,64,128]{3,2,1,0:T(8,128)S(1)} %copy-done.5, f32[2,25,65,128]{3,2,1,0:T(8,128)S(1)} %add_multiply_fusion.2, f32[2,25,64,129]{3,2,1,0:T(8,128)S(1)} %copy-done.7, f32[2,24,64,128]{3,2,1,0:T(8,128)} %fusion.12, f32[25,64,128]{2,1,0:T(8,128)S(1)} %copy-done.2), kind=kLoop, calls=%fused_computation.26 | loop fusion | flops 3686400 | bytes 12222464 | tf_op jit(solution)/shard_map/mul | solution.py:76
  145.0 1.9 %subtract_select_fusion = (f32[25,64,128]{2,1,0:T(8,128)}, f32[25,64,128]{2,1,0:T(8,128)}, f32[25,64,128]{2,1,0:T(8,128)}) fusion(f32[25]{0:T(128)S(1)} %get-tuple-element.31, f32[25]{0:T(128)S(1)} %get-tuple-element.32, s32[64,128]{1,0:T(8,128)S(1)} %copy-done.15, f32[2,25,64,128]{3,2,1,0:T(8,128)S(1)} %fusion.5), kind=kLoop, calls=%fused_computation.51 | loop fusion | flops 3276800 | bytes 4128968 | tf_op jit(solution)/shard_map/mul | solution.py:118
  (73 shorter events, 10.6 us)
Async XLA Ops:
  0.6 9.0 %copy-start.14 = (s32[64,128]{1,0:T(8,128)S(1)}, s32[64,128]{1,0:T(8,128)}, u32[]{:S(2)}) copy-start(s32[64,128]{1,0:T(8,128)} %param.13) | copy-start | bytes 98308
  0.6 9.1 %copy-start.13 = (f32[25,64,128]{2,1,0:T(8,128)S(1)}, f32[25,64,128]{2,1,0:T(8,128)}, u32[]{:S(2)}) copy-start(f32[25,64,128]{2,1,0:T(8,128)} %param.9) | copy-start | bytes 2457604
  2.2 42.8 %collective-permute-start.3 = (f32[25,1,128]{2,1,0:T(1,128)}, f32[25,1,128]{2,1,0:T(1,128)}, u32[]{:S(2)}, u32[]{:S(2)}) collective-permute-start(f32[25,1,128]{2,1,0:T(1,128)} %slice.173), channel_id=1, source_target_pairs={{0,1},{1,2},{2,3},{3,4},{4,5},{5,6},{6,7},{8,9},{9,10},{10,11},{11... | collective-permute-start | bytes 38408 | tf_op jit(solution)/shard_map/ppermute | solution.py:41
  7.1 32.8 %collective-permute-start = (f32[25,64,1]{1,0,2:T(8,128)S(1)}, f32[25,64,1]{1,0,2:T(8,128)}, u32[]{:S(2)}, u32[]{:S(2)}) collective-permute-start(f32[25,64,1]{1,0,2:T(8,128)S(1)} %copy.111), channel_id=1, source_target_pairs={{120,0},{0,8},{8,16},{16,24},{24,32},{32,40},{40,48},{48,56},{56,6... | collective-permute-start | bytes 19208 | tf_op jit(solution)/shard_map/ppermute | solution.py:35
  9.8 26.1 %copy-start = (f32[25,64,128]{2,1,0:T(8,128)}, f32[25,64,128]{2,1,0:T(8,128)S(1)}, u32[]{:S(2)}) copy-start(f32[25,64,128]{2,1,0:T(8,128)S(1)} %fusion.14) | copy-start | bytes 2457604
  14.1 59.4 %collective-permute-start.5 = (f32[2,25,2,128]{3,2,1,0:T(2,128)}, f32[2,25,2,128]{3,2,1,0:T(2,128)}, u32[]{:S(2)}, u32[]{:S(2)}) collective-permute-start(f32[2,25,2,128]{3,2,1,0:T(2,128)} %get-tuple-element.25), channel_id=1, source_target_pairs={{1,0},{2,1},{3,2},{4,3},{5,4},{6,5},{7,6},{9,8},{10,9},{11,10},{12... | collective-permute-start | bytes 153608 | tf_op jit(solution)/shard_map/ppermute | solution.py:27
  18.4 56.0 %collective-permute-start.4 = (f32[2,25,2,128]{3,2,1,0:T(2,128)}, f32[2,25,2,128]{3,2,1,0:T(2,128)}, u32[]{:S(2)}, u32[]{:S(2)}) collective-permute-start(f32[2,25,2,128]{3,2,1,0:T(2,128)} %get-tuple-element.26), channel_id=1, source_target_pairs={{0,1},{1,2},{2,3},{3,4},{4,5},{5,6},{6,7},{8,9},{9,10},{10,11},{11... | collective-permute-start | bytes 153608 | tf_op jit(solution)/shard_map/ppermute | solution.py:26
  22.2 28.6 %all-to-all-start = ((f32[16,1,800]{2,1,0:T(1,128)}), f32[16,1,800]{2,1,0:T(1,128)S(1)}, u32[]{:S(2)}, u32[]{:S(2)}) async-start(f32[16,1,800]{2,1,0:T(1,128)} %reshape.71), calls=%async_computation | async-start | bytes 114688 | tf_op jit(solution)/shard_map/all_to_all | solution.py:89
  34.0 15.0 %collective-permute-start.1 = (f32[2,25,64,2]{2,3,1,0:T(2,128)S(1)}, f32[2,25,64,2]{2,3,1,0:T(2,128)S(1)}, u32[]{:S(2)}, u32[]{:S(2)}) collective-permute-start(f32[2,25,64,2]{2,3,1,0:T(2,128)S(1)} %copy.95), channel_id=1, source_target_pairs={{0,8},{8,16},{16,24},{24,32},{32,40},{40,48},{48,56},{56,64},{64,7... | collective-permute-start | bytes 76808 | tf_op jit(solution)/shard_map/ppermute | solution.py:26
  35.9 1.4 copy-start.3
  37.3 2.0 %copy-start.9 = (f32[2,25,64,2]{3,2,1,0:T(8,128)S(1)}, f32[2,25,64,2]{3,2,1,0:T(8,128)}, u32[]{:S(2)}) copy-start(f32[2,25,64,2]{3,2,1,0:T(8,128)} %get-tuple-element.23) | copy-start | bytes 76804
  39.9 7.3 %collective-permute-start.2 = (f32[2,25,64,2]{2,3,1,0:T(2,128)S(1)}, f32[2,25,64,2]{2,3,1,0:T(2,128)S(1)}, u32[]{:S(2)}, u32[]{:S(2)}) collective-permute-start(f32[2,25,64,2]{2,3,1,0:T(2,128)S(1)} %copy.97), channel_id=1, source_target_pairs={{8,0},{16,8},{24,16},{32,24},{40,32},{48,40},{56,48},{64,56},{72,6... | collective-permute-start | bytes 76808 | tf_op jit(solution)/shard_map/ppermute | solution.py:27
  41.9 3.1 %copy-start.12 = (f32[25,64,128]{2,1,0:T(8,128)S(1)}, f32[25,64,128]{2,1,0:T(8,128)}, u32[]{:S(2)}) copy-start(f32[25,64,128]{2,1,0:T(8,128)} %param.12) | copy-start | bytes 2457604
  45.1 19.9 %copy-start.6 = (f32[25,64,129]{2,1,0:T(8,128)}, f32[25,64,129]{2,1,0:T(8,128)S(1)}, u32[]{:S(2)}) copy-start(f32[25,64,129]{2,1,0:T(8,128)S(1)} %get-tuple-element.21) | copy-start | bytes 2476804
  56.2 15.7 %all-to-all-start.1 = ((f32[16,1,800]{2,1,0:T(1,128)}), f32[16,1,800]{2,1,0:T(1,128)S(1)}, u32[]{:S(2)}, u32[]{:S(2)}) async-start(f32[16,1,800]{2,1,0:T(1,128)} %reshape.73), calls=%async_computation.1 | async-start | bytes 114688 | tf_op jit(solution)/shard_map/all_to_all | solution.py:90
  72.0 2.4 %copy-start.8 = (f32[25,65,128]{2,1,0:T(8,128)S(1)}, f32[25,65,128]{2,1,0:T(8,128)}, u32[]{:S(2)}) copy-start(f32[25,65,128]{2,1,0:T(8,128)} %get-tuple-element.27) | copy-start | bytes 2496004
  74.4 2.6 %copy-start.1 = (f32[25,64,128]{2,1,0:T(8,128)S(1)}, f32[25,64,128]{2,1,0:T(8,128)}, u32[]{:S(2)}) copy-start(f32[25,64,128]{2,1,0:T(8,128)} %copy-done) | copy-start | bytes 2457604
  74.4 2.6 %copy-start.4 = (f32[2,25,64,128]{3,2,1,0:T(8,128)S(1)}, f32[2,25,64,128]{3,2,1,0:T(8,128)}, u32[]{:S(2)}) copy-start(f32[2,25,64,128]{3,2,1,0:T(8,128)} %get-tuple-element.29) | copy-start | bytes 4915204
  74.4 2.6 %copy-start.10 = (f32[2,24,64,128]{3,2,1,0:T(8,128)S(1)}, f32[2,24,64,128]{3,2,1,0:T(8,128)}, u32[]{:S(2)}) copy-start(f32[2,24,64,128]{3,2,1,0:T(8,128)} %fusion.13) | copy-start | bytes 4718596
  82.8 56.0 %collective-permute-start.8 = (f32[2,25,2,128]{3,2,1,0:T(2,128)}, f32[2,25,2,128]{3,2,1,0:T(2,128)}, u32[]{:S(2)}, u32[]{:S(2)}) collective-permute-start(f32[2,25,2,128]{3,2,1,0:T(2,128)} %get-tuple-element.20), channel_id=1, source_target_pairs={{0,1},{1,2},{2,3},{3,4},{4,5},{5,6},{6,7},{8,9},{9,10},{10,11},{11... | collective-permute-start | bytes 153608 | tf_op jit(solution)/shard_map/ppermute | solution.py:26
  86.4 17.8 %copy-start.2 = (f32[25,64,128]{2,1,0:T(8,128)S(1)}, f32[25,64,128]{2,1,0:T(8,128)}, u32[]{:S(2)}) copy-start(f32[25,64,128]{2,1,0:T(8,128)} %copy-done) | copy-start | bytes 2457604
  88.7 49.3 %collective-permute-start.9 = (f32[2,25,2,128]{3,2,1,0:T(2,128)}, f32[2,25,2,128]{3,2,1,0:T(2,128)}, u32[]{:S(2)}, u32[]{:S(2)}) collective-permute-start(f32[2,25,2,128]{3,2,1,0:T(2,128)} %get-tuple-element.19), channel_id=1, source_target_pairs={{1,0},{2,1},{3,2},{4,3},{5,4},{6,5},{7,6},{9,8},{10,9},{11,10},{12... | collective-permute-start | bytes 153608 | tf_op jit(solution)/shard_map/ppermute | solution.py:27
  96.4 21.9 %all-to-all-start.2 = ((f32[16,1,800]{2,1,0:T(1,128)}), f32[16,1,800]{2,1,0:T(1,128)S(1)}, u32[]{:S(2)}, u32[]{:S(2)}) async-start(f32[16,1,800]{2,1,0:T(1,128)} %reshape.75), calls=%async_computation.2 | async-start | bytes 114688 | tf_op jit(solution)/shard_map/all_to_all | solution.py:89
  105.3 5.6 %copy-start.11 = (f32[24,64,128]{2,1,0:T(8,128)S(1)}, f32[24,64,128]{2,1,0:T(8,128)}, u32[]{:S(2)}) copy-start(f32[24,64,128]{2,1,0:T(8,128)} %add_multiply_fusion.4) | copy-start | bytes 2359300
  109.4 7.1 %collective-permute-start.6 = (f32[2,25,64,2]{2,3,1,0:T(2,128)S(1)}, f32[2,25,64,2]{2,3,1,0:T(2,128)S(1)}, u32[]{:S(2)}, u32[]{:S(2)}) collective-permute-start(f32[2,25,64,2]{2,3,1,0:T(2,128)S(1)} %copy.103), channel_id=1, source_target_pairs={{0,8},{8,16},{16,24},{24,32},{32,40},{40,48},{48,56},{56,64},{64,7... | collective-permute-start | bytes 76808 | tf_op jit(solution)/shard_map/ppermute | solution.py:26
  110.9 3.8 %collective-permute-start.7 = (f32[2,25,64,2]{2,3,1,0:T(2,128)S(1)}, f32[2,25,64,2]{2,3,1,0:T(2,128)S(1)}, u32[]{:S(2)}, u32[]{:S(2)}) collective-permute-start(f32[2,25,64,2]{2,3,1,0:T(2,128)S(1)} %copy.105), channel_id=1, source_target_pairs={{8,0},{16,8},{24,16},{32,24},{40,32},{48,40},{56,48},{64,56},{72,6... | collective-permute-start | bytes 76808 | tf_op jit(solution)/shard_map/ppermute | solution.py:27
  120.2 16.3 %all-to-all-start.3 = ((f32[16,1,800]{2,1,0:T(1,128)}), f32[16,1,800]{2,1,0:T(1,128)S(1)}, u32[]{:S(2)}, u32[]{:S(2)}) async-start(f32[16,1,800]{2,1,0:T(1,128)} %reshape.77), calls=%async_computation.3 | async-start | bytes 114688 | tf_op jit(solution)/shard_map/all_to_all | solution.py:90
  138.8 2.8 %copy-start.5 = (f32[2,25,64,128]{3,2,1,0:T(8,128)S(1)}, f32[2,25,64,128]{3,2,1,0:T(8,128)}, u32[]{:S(2)}) copy-start(f32[2,25,64,128]{3,2,1,0:T(8,128)} %get-tuple-element.15) | copy-start | bytes 4915204
  138.8 3.0 %copy-start.7 = (f32[2,25,64,129]{3,2,1,0:T(8,128)S(1)}, f32[2,25,64,129]{3,2,1,0:T(8,128)}, u32[]{:S(2)}) copy-start(f32[2,25,64,129]{3,2,1,0:T(8,128)} %add_multiply_fusion) | copy-start | bytes 4953604
  141.8 3.2 %copy-start.15 = (s32[64,128]{1,0:T(8,128)S(1)}, s32[64,128]{1,0:T(8,128)}, u32[]{:S(2)}) copy-start(s32[64,128]{1,0:T(8,128)} %param.13) | copy-start | bytes 98308
where the time goes:
time: 148 us; the launch traced here: 147 us
  starting transfers between devices  55.4 us (37%)
  other arithmetic  51.2 us (35%)
  local copies, waits for them, and re-layouts  38.8 us (26%)
    add x4, other arithmetic, divergence(): flux + jnp.abs(velocity) * (ahead_far - behind_far - 3.0 * (ahead - behin...  19.6 us
    all_to_all x2, starting transfers between devices, extend_tracers(): lax.all_to_all(spread[:, :, :, ::-1, :], 'lon', split_axis=3, concat_axis...  17.8 us
    all_to_all x2, starting transfers between devices, extend_tracers(): lax.all_to_all(pieces, 'lon', split_axis=3, concat_axis=3, tiled=True)  15.3 us
    unnamed x45, local copies, waits for them, and re-layouts  11.2 us
    ppermute x4, starting transfers between devices, extended_2(): after = lax.ppermute(leading, axis, down)  9.51 us
    slice x6, local copies, waits for them, and re-layouts, extended_2(): leading = lax.slice_in_dim(value, 0, width, axis=dim)  8.48 us
    ppermute x4, starting transfers between devices, extended_2(): before = lax.ppermute(last, axis, up)  7.17 us
    slice x4, local copies, waits for them, and re-layouts, extended_2(): last = lax.slice_in_dim(value, length - width, length, axis=dim)  5.87 us
  transfers between devices with their start and end apart: 14, of which 1 were waited for; matrix products, arithmetic and copies ran while one was open for 48% of the time, Pallas kernels for 0%

commit v1 on v0

--- a/solution.py
+++ b/solution.py
@@ -86,7 +86,10 @@
     pieces = edge_rows.reshape(
         edge_rows.shape[0], edge_rows.shape[1], 2, cycle_size, columns // cycle_size
     )
-    spread = lax.all_to_all(pieces, "lon", split_axis=3, concat_axis=3, tiled=True)
+    spread = jnp.concatenate(
+        lax.all_to_all(jnp.stack(jnp.split(pieces, lax.axis_size("lon"), axis=3)), "lon", 0, 0),
+        axis=3,
+    )
     returned = lax.all_to_all(
         spread[:, :, :, ::-1, :], "lon", split_axis=3, concat_axis=3, tiled=True
     )

time: 148 us -> 147 us (level)
  local copies, waits for them, and re-layouts: 38.8 us -> 37.3 us
    unnamed x45 -> x75, local copies, waits for them, and re-layouts: 11.2 us -> 9.61 us
  transfers between devices with their start and end apart: 14 -> 14, of which waited for: 1 -> 1; matrix products, arithmetic and copies ran while one was open for 48% -> 47% of each run, Pallas kernels for 0% -> 0%
where the time goes in v1:
time: 147 us; the launch traced here: 146 us
  starting transfers between devices  55.4 us (38%)
  other arithmetic  51.3 us (35%)
  local copies, waits for them, and re-layouts  37.3 us (25%)
    add x4, other arithmetic, divergence(): flux + jnp.abs(velocity) * (ahead_far - behind_far - 3.0 * (ahead - behin...  19.5 us
    all_to_all x2, starting transfers between devices, extend_tracers(): lax.all_to_all(spread[:, :, :, ::-1, :], 'lon', split_axis=3, concat_axis...  17.8 us
    all_to_all x2, starting transfers between devices, extend_tracers(): lax.all_to_all(jnp.stack(jnp.split(pieces, lax.axis_size('lon'), axis=3))...  15.3 us
    unnamed x75, local copies, waits for them, and re-layouts  9.61 us
    ppermute x4, starting transfers between devices, extended_2(): after = lax.ppermute(leading, axis, down)  9.51 us
    slice x6, local copies, waits for them, and re-layouts, extended_2(): leading = lax.slice_in_dim(value, 0, width, axis=dim)  8.51 us
    ppermute x4, starting transfers between devices, extended_2(): before = lax.ppermute(last, axis, up)  7.17 us
    slice x4, local copies, waits for them, and re-layouts, extended_2(): last = lax.slice_in_dim(value, length - width, length, axis=dim)  5.87 us
  transfers between devices with their start and end apart: 14, of which 1 were waited for; matrix products, arithmetic and copies ran while one was open for 47% of the time, Pallas kernels for 0%

profile of v1, /device:TPU:25, one launch (start us, length us, event | category | flops | bytes accessed | tf_op | source)
XLA Modules:
  0.0 145.7 jit_solution(254289906382361210)
XLA Ops:
  0.7 1.6 %slice.173 = f32[25,1,128]{2,1,0:T(1,128)} slice(f32[25,64,128]{2,1,0:T(8,128)} %param.12), slice={[0:25], [63:64], [0:128]} | slice | bytes 25600 | tf_op jit(solution)/shard_map/slice | solution.py:115
  2.2 3.1 %collective-permute-start.3 = (f32[25,1,128]{2,1,0:T(1,128)}, f32[25,1,128]{2,1,0:T(1,128)}, u32[]{:S(2)}, u32[]{:S(2)}) collective-permute-start(f32[25,1,128]{2,1,0:T(1,128)} %slice.173), channel_id=1, source_target_pairs={{0,1},{1,2},{2,3},{3,4},{4,5},{5,6},{6,7},{8,9},{9,10},{10,11},{11... | collective-permute-start | bytes 38408 | tf_op jit(solution)/shard_map/ppermute | solution.py:41
  5.4 1.4 slice.164
  7.1 2.5 %collective-permute-start = (f32[25,64,1]{1,0,2:T(8,128)S(1)}, f32[25,64,1]{1,0,2:T(8,128)}, u32[]{:S(2)}, u32[]{:S(2)}) collective-permute-start(f32[25,64,1]{1,0,2:T(8,128)S(1)} %copy.287), channel_id=1, source_target_pairs={{120,0},{0,8},{8,16},{16,24},{24,32},{32,40},{40,48},{48,56},{56,6... | collective-permute-start | bytes 19208 | tf_op jit(solution)/shard_map/ppermute | solution.py:35
  9.8 3.7 %maximum_multiply_fusion.1 = (f32[2,25,64,128]{3,2,1,0:T(8,128)}, f32[2,25,64,128]{3,2,1,0:T(8,128)S(1)}) fusion(f32[1,25,64,128]{3,2,1,0:T(8,128)S(1)} %bitcast.276, f32[1,25,64,128]{3,2,1,0:T(8,128)} %bitcast.277, f32[25,64,128]{2,1,0:T(8,128)S(1)} %fusion.14, f32[1,25,64,128]{3,2,1,0:T(8,128)} %bitcast.278, f32[1,25,64,128]{3,2,1,0:T(8,128)} %bitcast.279), kind=kLoop, calls=%fused_computation.37 | loop fusion | flops 1638400 | bytes 7372800 | tf_op jit(solution)/shard_map/mul | solution.py:111
  14.1 4.3 %collective-permute-start.5 = (f32[2,25,2,128]{3,2,1,0:T(2,128)}, f32[2,25,2,128]{3,2,1,0:T(2,128)}, u32[]{:S(2)}, u32[]{:S(2)}) collective-permute-start(f32[2,25,2,128]{3,2,1,0:T(2,128)} %get-tuple-element.25), channel_id=1, source_target_pairs={{1,0},{2,1},{3,2},{4,3},{5,4},{6,5},{7,6},{9,8},{10,9},{11,10},{12... | collective-permute-start | bytes 153608 | tf_op jit(solution)/shard_map/ppermute | solution.py:27
  18.4 1.9 %collective-permute-start.4 = (f32[2,25,2,128]{3,2,1,0:T(2,128)}, f32[2,25,2,128]{3,2,1,0:T(2,128)}, u32[]{:S(2)}, u32[]{:S(2)}) collective-permute-start(f32[2,25,2,128]{3,2,1,0:T(2,128)} %get-tuple-element.26), channel_id=1, source_target_pairs={{0,1},{1,2},{2,3},{3,4},{4,5},{5,6},{6,7},{8,9},{9,10},{10,11},{11... | collective-permute-start | bytes 153608 | tf_op jit(solution)/shard_map/ppermute | solution.py:26
  20.3 0.9 copy.247
  21.5 0.9 reshape.87
  22.3 7.6 %all-to-all-start = ((f32[16,1,800]{2,1,0:T(1,128)}), f32[16,1,800]{2,1,0:T(1,128)S(1)}, u32[]{:S(2)}, u32[]{:S(2)}) async-start(f32[16,1,800]{2,1,0:T(1,128)} %reshape.87), calls=%async_computation | async-start | bytes 114688 | tf_op jit(solution)/shard_map/all_to_all | solution.py:90
  29.9 2.3 %fusion.34 = (f32[2,25,64,2]{3,2,1,0:T(8,128)}, f32[2,25,64,2]{3,2,1,0:T(8,128)}) fusion(f32[2,25,64,128]{3,2,1,0:T(8,128)S(1)} %get-tuple-element.30), kind=kLoop, calls=%fused_computation.147 | loop fusion | bytes 102400 | tf_op jit(solution)/shard_map/slice | solution.py:25
  32.2 2.0 %copy.243 = f32[2,25,64,2]{2,3,1,0:T(2,128)S(1)} copy(f32[2,25,64,2]{3,2,1,0:T(8,128)} %get-tuple-element.24) | data formatting | bytes 51200 | tf_op jit(solution)/shard_map/slice | solution.py:24
  34.2 1.5 %collective-permute-start.1 = (f32[2,25,64,2]{2,3,1,0:T(2,128)S(1)}, f32[2,25,64,2]{2,3,1,0:T(2,128)S(1)}, u32[]{:S(2)}, u32[]{:S(2)}) collective-permute-start(f32[2,25,64,2]{2,3,1,0:T(2,128)S(1)} %copy.243), channel_id=1, source_target_pairs={{0,8},{8,16},{16,24},{24,32},{32,40},{40,48},{48,56},{56,64},{64,7... | collective-permute-start | bytes 76808 | tf_op jit(solution)/shard_map/ppermute | solution.py:26
  36.4 1.2 copy-done.3
  37.5 1.5 %fusion.13 = f32[2,24,64,128]{3,2,1,0:T(8,128)} fusion(f32[2,25,64,128]{3,2,1,0:T(8,128)S(1)} %copy-done.3, f32[24,64,128]{2,1,0:T(8,128)S(1)} %add_multiply_fusion.5), kind=kLoop, calls=%fused_computation.43 | loop fusion | flops 786432 | bytes 5505024 | tf_op jit(solution)/shard_map/mul | solution.py:68
  40.2 1.9 %copy.242 = f32[25,64,1]{2,1,0:T(8,128)} copy(f32[25,64,1]{1,0,2:T(8,128)} %collective-permute-done) | data formatting | bytes 12800 | tf_op jit(solution)/shard_map/ppermute | solution.py:35
  42.1 3.1 %pad_maximum_fusion.8 = (f32[25,64,129]{2,1,0:T(8,128)S(1)}, f32[25,64,129]{2,1,0:T(8,128)}) fusion(f32[25,64,128]{2,1,0:T(8,128)} %param.11, f32[25,64,1]{2,1,0:T(8,128)} %copy.242), kind=kLoop, calls=%fused_computation.38 | loop fusion | flops 412800 | bytes 2476800 | tf_op jit(solution)/shard_map/concatenate | solution.py:114
  45.3 2.1 %pad_maximum_fusion.9 = (f32[25,65,128]{2,1,0:T(8,128)}, f32[25,65,128]{2,1,0:T(8,128)}) fusion(f32[25,64,128]{2,1,0:T(8,128)S(1)} %copy-done.12, f32[25,1,128]{2,1,0:T(1,128)} %collective-permute-done.3), kind=kLoop, calls=%fused_computation.44 | loop fusion | flops 416000 | bytes 2496000 | tf_op jit(solution)/shard_map/concatenate | solution.py:116
  47.4 1.7 %copy.246 = f32[2,25,64,2]{3,2,1,0:T(8,128)} copy(f32[2,25,64,2]{2,3,1,0:T(2,128)S(1)} %collective-permute-done.2) | data formatting | bytes 51200 | tf_op jit(solution)/shard_map/ppermute | solution.py:27
  49.1 1.8 %copy.244 = f32[2,25,64,2]{3,2,1,0:T(8,128)} copy(f32[2,25,64,2]{2,3,1,0:T(2,128)S(1)} %collective-permute-done.1) | data formatting | bytes 51200 | tf_op jit(solution)/shard_map/ppermute | solution.py:26
  51.4 1.4 reduce
  52.8 1.1 reshape.88
  54.0 0.9 reshape.89
  54.8 8.7 %all-to-all-start.1 = ((f32[16,1,800]{2,1,0:T(1,128)}), f32[16,1,800]{2,1,0:T(1,128)S(1)}, u32[]{:S(2)}, u32[]{:S(2)}) async-start(f32[16,1,800]{2,1,0:T(1,128)} %reshape.89), calls=%async_computation.1 | async-start | bytes 114688 | tf_op jit(solution)/shard_map/all_to_all | solution.py:93
  63.6 7.0 %add_multiply_fusion.1 = f32[2,25,64,129]{3,2,1,0:T(8,128)} fusion(f32[2,25,64,128]{3,2,1,0:T(8,128)S(1)} %get-tuple-element.30, f32[2,25,64,2]{3,2,1,0:T(8,128)} %copy.244, f32[2,25,64,2]{3,2,1,0:T(8,128)} %copy.246, f32[25,64,129]{2,1,0:T(8,128)} %get-tuple-element.22, f32[25,64,129]{2,1,0:T(8,128)S(1)} %get-tuple-element.21), kind=kLoop, calls=%fused_computation.9 | loop fusion | flops 6604800 | bytes 4992000 | tf_op jit(solution)/shard_map/add | solution.py:58
  70.5 0.8 reduce.1
  72.1 0.8 broadcast_select_fusion.1
  73.0 2.6 %add_multiply_fusion.3 = f32[2,25,65,128]{3,2,1,0:T(8,128)S(1)} fusion(f32[2,25,64,128]{3,2,1,0:T(8,128)S(1)} %get-tuple-element.30, f32[2,25,2,128]{3,2,1,0:T(2,128)} %collective-permute-done.4, f32[2,25,2,128]{3,2,1,0:T(2,128)S(1)} %broadcast_select_fusion.1, f32[25,65,128]{2,1,0:T(8,128)} %get-tuple-element.28, f32[25,65,128]{2,1,0:T(8,128)S(1)} %copy-done.8), kind=kLoop, calls=%fused_computation.19 | loop fusion | flops 6656000 | bytes 5068800 | tf_op jit(solution)/shard_map/add | solution.py:58
  75.6 5.1 %multiply_add_fusion = (f32[2,25,64,128]{3,2,1,0:T(8,128)}, f32[2,25,64,128]{3,2,1,0:T(8,128)S(1)}) fusion(f32[2,25,64,128]{3,2,1,0:T(8,128)S(1)} %get-tuple-element.30, f32[2,25,64,128]{3,2,1,0:T(8,128)S(1)} %copy-done.4, f32[25,64,128]{2,1,0:T(8,128)S(1)} %copy-done.1, f32[2,24,64,128]{3,2,1,0:T(8,128)S(1)} %copy-done.10, ...), kind=kLoop, calls=%fused_computation.39 | loop fusion | flops 5734400 | bytes 15499264 | tf_op jit(solution)/shard_map/add | solution.py:77
  81.4 2.2 %collective-permute-start.8 = (f32[2,25,2,128]{3,2,1,0:T(2,128)}, f32[2,25,2,128]{3,2,1,0:T(2,128)}, u32[]{:S(2)}, u32[]{:S(2)}) collective-permute-start(f32[2,25,2,128]{3,2,1,0:T(2,128)} %get-tuple-element.20), channel_id=1, source_target_pairs={{0,1},{1,2},{2,3},{3,4},{4,5},{5,6},{6,7},{8,9},{9,10},{10,11},{11... | collective-permute-start | bytes 153608 | tf_op jit(solution)/shard_map/ppermute | solution.py:26
  83.6 0.9 copy.269
  85.0 2.3 %fusion.32 = (f32[2,25,64,2]{3,2,1,0:T(8,128)}, f32[2,25,64,2]{3,2,1,0:T(8,128)}) fusion(f32[2,25,64,128]{3,2,1,0:T(8,128)S(1)} %get-tuple-element.16), kind=kLoop, calls=%fused_computation.145 | loop fusion | bytes 102400 | tf_op jit(solution)/shard_map/slice | solution.py:25
  87.3 5.2 %collective-permute-start.9 = (f32[2,25,2,128]{3,2,1,0:T(2,128)}, f32[2,25,2,128]{3,2,1,0:T(2,128)}, u32[]{:S(2)}, u32[]{:S(2)}) collective-permute-start(f32[2,25,2,128]{3,2,1,0:T(2,128)} %get-tuple-element.19), channel_id=1, source_target_pairs={{1,0},{2,1},{3,2},{4,3},{5,4},{6,5},{7,6},{9,8},{10,9},{11,10},{12... | collective-permute-start | bytes 153608 | tf_op jit(solution)/shard_map/ppermute | solution.py:27
  93.4 1.8 %reshape.91 = f32[16,1,800]{2,1,0:T(1,128)} reshape(f32[16,1,2,2,8,25]{5,4,3,2,1,0:T(8,128)} %bitcast.281) | data formatting | bytes 102400
  95.2 7.8 %all-to-all-start.2 = ((f32[16,1,800]{2,1,0:T(1,128)}), f32[16,1,800]{2,1,0:T(1,128)S(1)}, u32[]{:S(2)}, u32[]{:S(2)}) async-start(f32[16,1,800]{2,1,0:T(1,128)} %reshape.91), calls=%async_computation.2 | async-start | bytes 114688 | tf_op jit(solution)/shard_map/all_to_all | solution.py:90
  103.0 1.1 add_multiply_fusion.4
  104.1 2.1 %copy.267 = f32[2,25,64,2]{2,3,1,0:T(2,128)S(1)} copy(f32[2,25,64,2]{3,2,1,0:T(8,128)} %get-tuple-element.17) | data formatting | bytes 51200 | tf_op jit(solution)/shard_map/slice | solution.py:25
  106.2 2.0 %copy.265 = f32[2,25,64,2]{2,3,1,0:T(2,128)S(1)} copy(f32[2,25,64,2]{3,2,1,0:T(8,128)} %get-tuple-element.18) | data formatting | bytes 51200 | tf_op jit(solution)/shard_map/slice | solution.py:24
  108.2 1.5 %collective-permute-start.6 = (f32[2,25,64,2]{2,3,1,0:T(2,128)S(1)}, f32[2,25,64,2]{2,3,1,0:T(2,128)S(1)}, u32[]{:S(2)}, u32[]{:S(2)}) collective-permute-start(f32[2,25,64,2]{2,3,1,0:T(2,128)S(1)} %copy.265), channel_id=1, source_target_pairs={{0,8},{8,16},{16,24},{24,32},{32,40},{40,48},{48,56},{56,64},{64,7... | collective-permute-start | bytes 76808 | tf_op jit(solution)/shard_map/ppermute | solution.py:26
  109.7 3.6 %fusion.12 = f32[2,24,64,128]{3,2,1,0:T(8,128)} fusion(f32[2,25,64,128]{3,2,1,0:T(8,128)} %get-tuple-element.15, f32[24,64,128]{2,1,0:T(8,128)S(1)} %copy-done.11), kind=kLoop, calls=%fused_computation.41 | loop fusion | flops 786432 | bytes 5505024 | tf_op jit(solution)/shard_map/mul | solution.py:68
  113.5 1.7 %copy.268 = f32[2,25,64,2]{3,2,1,0:T(8,128)} copy(f32[2,25,64,2]{2,3,1,0:T(2,128)S(1)} %collective-permute-done.7) | data formatting | bytes 51200 | tf_op jit(solution)/shard_map/ppermute | solution.py:27
  115.3 1.8 %copy.266 = f32[2,25,64,2]{3,2,1,0:T(8,128)} copy(f32[2,25,64,2]{2,3,1,0:T(2,128)S(1)} %collective-permute-done.6) | data formatting | bytes 51200 | tf_op jit(solution)/shard_map/ppermute | solution.py:26
  118.2 0.9 reshape.93
  119.0 9.1 %all-to-all-start.3 = ((f32[16,1,800]{2,1,0:T(1,128)}), f32[16,1,800]{2,1,0:T(1,128)S(1)}, u32[]{:S(2)}, u32[]{:S(2)}) async-start(f32[16,1,800]{2,1,0:T(1,128)} %reshape.93), calls=%async_computation.3 | async-start | bytes 114688 | tf_op jit(solution)/shard_map/all_to_all | solution.py:93
  128.1 7.2 %add_multiply_fusion = f32[2,25,64,129]{3,2,1,0:T(8,128)} fusion(f32[2,25,64,128]{3,2,1,0:T(8,128)S(1)} %get-tuple-element.16, f32[2,25,64,2]{3,2,1,0:T(8,128)} %copy.266, f32[2,25,64,2]{3,2,1,0:T(8,128)} %copy.268, f32[25,64,129]{2,1,0:T(8,128)} %get-tuple-element.22, f32[25,64,129]{2,1,0:T(8,128)} %copy-done.6), kind=kLoop, calls=%fused_computation.8 | loop fusion | flops 6604800 | bytes 4992000 | tf_op jit(solution)/shard_map/add | solution.py:58
  137.7 2.7 %add_multiply_fusion.2 = f32[2,25,65,128]{3,2,1,0:T(8,128)S(1)} fusion(f32[2,25,64,128]{3,2,1,0:T(8,128)S(1)} %get-tuple-element.16, f32[2,25,2,128]{3,2,1,0:T(2,128)} %collective-permute-done.8, f32[2,25,2,128]{3,2,1,0:T(2,128)S(1)} %broadcast_select_fusion, f32[25,65,128]{2,1,0:T(8,128)} %get-tuple-element.28, f32[25,65,128]{2,1,0:T(8,128)} %get-tuple-element.27), kind=kLoop, calls=%fused_computation.18 | loop fusion | flops 6656000 | bytes 5068800 | tf_op jit(solution)/shard_map/add | solution.py:58
  140.7 3.2 %fusion.5 = f32[2,25,64,128]{3,2,1,0:T(8,128)S(1)} fusion(f32[2,25,64,128]{3,2,1,0:T(8,128)S(1)} %copy-done.5, f32[2,25,65,128]{3,2,1,0:T(8,128)S(1)} %add_multiply_fusion.2, f32[2,25,64,129]{3,2,1,0:T(8,128)S(1)} %copy-done.7, f32[2,24,64,128]{3,2,1,0:T(8,128)} %fusion.12, f32[25,64,128]{2,1,0:T(8,128)S(1)} %copy-done.2), kind=kLoop, calls=%fused_computation.26 | loop fusion | flops 3686400 | bytes 12222464 | tf_op jit(solution)/shard_map/mul | solution.py:76
  143.9 1.9 %subtract_select_fusion = (f32[25,64,128]{2,1,0:T(8,128)}, f32[25,64,128]{2,1,0:T(8,128)}, f32[25,64,128]{2,1,0:T(8,128)}) fusion(f32[25]{0:T(128)S(1)} %get-tuple-element.31, f32[25]{0:T(128)S(1)} %get-tuple-element.32, s32[64,128]{1,0:T(8,128)S(1)} %copy-done.16, f32[2,25,64,128]{3,2,1,0:T(8,128)S(1)} %fusion.5), kind=kLoop, calls=%fused_computation.51 | loop fusion | flops 3276800 | bytes 4128968 | tf_op jit(solution)/shard_map/mul | solution.py:121
  (107 shorter events, 10.1 us)
Async XLA Ops:
  0.6 9.0 %copy-start.15 = (s32[64,128]{1,0:T(8,128)S(1)}, s32[64,128]{1,0:T(8,128)}, u32[]{:S(2)}) copy-start(s32[64,128]{1,0:T(8,128)} %param.13) | copy-start | bytes 98308
  0.6 9.1 %copy-start.13 = (f32[25,64,128]{2,1,0:T(8,128)S(1)}, f32[25,64,128]{2,1,0:T(8,128)}, u32[]{:S(2)}) copy-start(f32[25,64,128]{2,1,0:T(8,128)} %param.9) | copy-start | bytes 2457604
  2.2 43.0 %collective-permute-start.3 = (f32[25,1,128]{2,1,0:T(1,128)}, f32[25,1,128]{2,1,0:T(1,128)}, u32[]{:S(2)}, u32[]{:S(2)}) collective-permute-start(f32[25,1,128]{2,1,0:T(1,128)} %slice.173), channel_id=1, source_target_pairs={{0,1},{1,2},{2,3},{3,4},{4,5},{5,6},{6,7},{8,9},{9,10},{10,11},{11... | collective-permute-start | bytes 38408 | tf_op jit(solution)/shard_map/ppermute | solution.py:41
  7.1 32.9 %collective-permute-start = (f32[25,64,1]{1,0,2:T(8,128)S(1)}, f32[25,64,1]{1,0,2:T(8,128)}, u32[]{:S(2)}, u32[]{:S(2)}) collective-permute-start(f32[25,64,1]{1,0,2:T(8,128)S(1)} %copy.287), channel_id=1, source_target_pairs={{120,0},{0,8},{8,16},{16,24},{24,32},{32,40},{40,48},{48,56},{56,6... | collective-permute-start | bytes 19208 | tf_op jit(solution)/shard_map/ppermute | solution.py:35
  9.8 26.3 %copy-start = (f32[25,64,128]{2,1,0:T(8,128)}, f32[25,64,128]{2,1,0:T(8,128)S(1)}, u32[]{:S(2)}) copy-start(f32[25,64,128]{2,1,0:T(8,128)S(1)} %fusion.14) | copy-start | bytes 2457604
  14.1 58.0 %collective-permute-start.5 = (f32[2,25,2,128]{3,2,1,0:T(2,128)}, f32[2,25,2,128]{3,2,1,0:T(2,128)}, u32[]{:S(2)}, u32[]{:S(2)}) collective-permute-start(f32[2,25,2,128]{3,2,1,0:T(2,128)} %get-tuple-element.25), channel_id=1, source_target_pairs={{1,0},{2,1},{3,2},{4,3},{5,4},{6,5},{7,6},{9,8},{10,9},{11,10},{12... | collective-permute-start | bytes 153608 | tf_op jit(solution)/shard_map/ppermute | solution.py:27
  18.4 54.6 %collective-permute-start.4 = (f32[2,25,2,128]{3,2,1,0:T(2,128)}, f32[2,25,2,128]{3,2,1,0:T(2,128)}, u32[]{:S(2)}, u32[]{:S(2)}) collective-permute-start(f32[2,25,2,128]{3,2,1,0:T(2,128)} %get-tuple-element.26), channel_id=1, source_target_pairs={{0,1},{1,2},{2,3},{3,4},{4,5},{5,6},{6,7},{8,9},{9,10},{10,11},{11... | collective-permute-start | bytes 153608 | tf_op jit(solution)/shard_map/ppermute | solution.py:26
  22.3 28.6 %all-to-all-start = ((f32[16,1,800]{2,1,0:T(1,128)}), f32[16,1,800]{2,1,0:T(1,128)S(1)}, u32[]{:S(2)}, u32[]{:S(2)}) async-start(f32[16,1,800]{2,1,0:T(1,128)} %reshape.87), calls=%async_computation | async-start | bytes 114688 | tf_op jit(solution)/shard_map/all_to_all | solution.py:90
  34.2 15.0 %collective-permute-start.1 = (f32[2,25,64,2]{2,3,1,0:T(2,128)S(1)}, f32[2,25,64,2]{2,3,1,0:T(2,128)S(1)}, u32[]{:S(2)}, u32[]{:S(2)}) collective-permute-start(f32[2,25,64,2]{2,3,1,0:T(2,128)S(1)} %copy.243), channel_id=1, source_target_pairs={{0,8},{8,16},{16,24},{24,32},{32,40},{40,48},{48,56},{56,64},{64,7... | collective-permute-start | bytes 76808 | tf_op jit(solution)/shard_map/ppermute | solution.py:26
  36.1 1.4 copy-start.3
  37.5 2.0 %copy-start.9 = (f32[2,25,64,2]{3,2,1,0:T(8,128)S(1)}, f32[2,25,64,2]{3,2,1,0:T(8,128)}, u32[]{:S(2)}) copy-start(f32[2,25,64,2]{3,2,1,0:T(8,128)} %get-tuple-element.23) | copy-start | bytes 76804
  40.1 7.3 %collective-permute-start.2 = (f32[2,25,64,2]{2,3,1,0:T(2,128)S(1)}, f32[2,25,64,2]{2,3,1,0:T(2,128)S(1)}, u32[]{:S(2)}, u32[]{:S(2)}) collective-permute-start(f32[2,25,64,2]{2,3,1,0:T(2,128)S(1)} %copy.245), channel_id=1, source_target_pairs={{8,0},{16,8},{24,16},{32,24},{40,32},{48,40},{56,48},{64,56},{72,6... | collective-permute-start | bytes 76808 | tf_op jit(solution)/shard_map/ppermute | solution.py:27
  42.1 3.1 %copy-start.12 = (f32[25,64,128]{2,1,0:T(8,128)S(1)}, f32[25,64,128]{2,1,0:T(8,128)}, u32[]{:S(2)}) copy-start(f32[25,64,128]{2,1,0:T(8,128)} %param.12) | copy-start | bytes 2457604
  45.3 18.3 %copy-start.6 = (f32[25,64,129]{2,1,0:T(8,128)}, f32[25,64,129]{2,1,0:T(8,128)S(1)}, u32[]{:S(2)}) copy-start(f32[25,64,129]{2,1,0:T(8,128)S(1)} %get-tuple-element.21) | copy-start | bytes 2476804
  54.8 15.7 %all-to-all-start.1 = ((f32[16,1,800]{2,1,0:T(1,128)}), f32[16,1,800]{2,1,0:T(1,128)S(1)}, u32[]{:S(2)}, u32[]{:S(2)}) async-start(f32[16,1,800]{2,1,0:T(1,128)} %reshape.89), calls=%async_computation.1 | async-start | bytes 114688 | tf_op jit(solution)/shard_map/all_to_all | solution.py:93
  70.5 2.4 %copy-start.8 = (f32[25,65,128]{2,1,0:T(8,128)S(1)}, f32[25,65,128]{2,1,0:T(8,128)}, u32[]{:S(2)}) copy-start(f32[25,65,128]{2,1,0:T(8,128)} %get-tuple-element.27) | copy-start | bytes 2496004
  73.0 2.6 %copy-start.1 = (f32[25,64,128]{2,1,0:T(8,128)S(1)}, f32[25,64,128]{2,1,0:T(8,128)}, u32[]{:S(2)}) copy-start(f32[25,64,128]{2,1,0:T(8,128)} %copy-done) | copy-start | bytes 2457604
  73.0 2.6 %copy-start.4 = (f32[2,25,64,128]{3,2,1,0:T(8,128)S(1)}, f32[2,25,64,128]{3,2,1,0:T(8,128)}, u32[]{:S(2)}) copy-start(f32[2,25,64,128]{3,2,1,0:T(8,128)} %get-tuple-element.29) | copy-start | bytes 4915204
  73.0 2.6 %copy-start.10 = (f32[2,24,64,128]{3,2,1,0:T(8,128)S(1)}, f32[2,24,64,128]{3,2,1,0:T(8,128)}, u32[]{:S(2)}) copy-start(f32[2,24,64,128]{3,2,1,0:T(8,128)} %fusion.13) | copy-start | bytes 4718596
  81.4 56.2 %collective-permute-start.8 = (f32[2,25,2,128]{3,2,1,0:T(2,128)}, f32[2,25,2,128]{3,2,1,0:T(2,128)}, u32[]{:S(2)}, u32[]{:S(2)}) collective-permute-start(f32[2,25,2,128]{3,2,1,0:T(2,128)} %get-tuple-element.20), channel_id=1, source_target_pairs={{0,1},{1,2},{2,3},{3,4},{4,5},{5,6},{6,7},{8,9},{9,10},{10,11},{11... | collective-permute-start | bytes 153608 | tf_op jit(solution)/shard_map/ppermute | solution.py:26
  85.0 18.0 %copy-start.2 = (f32[25,64,128]{2,1,0:T(8,128)S(1)}, f32[25,64,128]{2,1,0:T(8,128)}, u32[]{:S(2)}) copy-start(f32[25,64,128]{2,1,0:T(8,128)} %copy-done) | copy-start | bytes 2457604
  87.3 49.5 %collective-permute-start.9 = (f32[2,25,2,128]{3,2,1,0:T(2,128)}, f32[2,25,2,128]{3,2,1,0:T(2,128)}, u32[]{:S(2)}, u32[]{:S(2)}) collective-permute-start(f32[2,25,2,128]{3,2,1,0:T(2,128)} %get-tuple-element.19), channel_id=1, source_target_pairs={{1,0},{2,1},{3,2},{4,3},{5,4},{6,5},{7,6},{9,8},{10,9},{11,10},{12... | collective-permute-start | bytes 153608 | tf_op jit(solution)/shard_map/ppermute | solution.py:27
  92.7 0.7 copy-start.14
  95.2 21.8 %all-to-all-start.2 = ((f32[16,1,800]{2,1,0:T(1,128)}), f32[16,1,800]{2,1,0:T(1,128)S(1)}, u32[]{:S(2)}, u32[]{:S(2)}) async-start(f32[16,1,800]{2,1,0:T(1,128)} %reshape.91), calls=%async_computation.2 | async-start | bytes 114688 | tf_op jit(solution)/shard_map/all_to_all | solution.py:90
  104.1 5.6 %copy-start.11 = (f32[24,64,128]{2,1,0:T(8,128)S(1)}, f32[24,64,128]{2,1,0:T(8,128)}, u32[]{:S(2)}) copy-start(f32[24,64,128]{2,1,0:T(8,128)} %add_multiply_fusion.4) | copy-start | bytes 2359300
  108.2 7.1 %collective-permute-start.6 = (f32[2,25,64,2]{2,3,1,0:T(2,128)S(1)}, f32[2,25,64,2]{2,3,1,0:T(2,128)S(1)}, u32[]{:S(2)}, u32[]{:S(2)}) collective-permute-start(f32[2,25,64,2]{2,3,1,0:T(2,128)S(1)} %copy.265), channel_id=1, source_target_pairs={{0,8},{8,16},{16,24},{24,32},{32,40},{40,48},{48,56},{56,64},{64,7... | collective-permute-start | bytes 76808 | tf_op jit(solution)/shard_map/ppermute | solution.py:26
  109.7 3.8 %collective-permute-start.7 = (f32[2,25,64,2]{2,3,1,0:T(2,128)S(1)}, f32[2,25,64,2]{2,3,1,0:T(2,128)S(1)}, u32[]{:S(2)}, u32[]{:S(2)}) collective-permute-start(f32[2,25,64,2]{2,3,1,0:T(2,128)S(1)} %copy.267), channel_id=1, source_target_pairs={{8,0},{16,8},{24,16},{32,24},{40,32},{48,40},{56,48},{64,56},{72,6... | collective-permute-start | bytes 76808 | tf_op jit(solution)/shard_map/ppermute | solution.py:27
  119.0 16.3 %all-to-all-start.3 = ((f32[16,1,800]{2,1,0:T(1,128)}), f32[16,1,800]{2,1,0:T(1,128)S(1)}, u32[]{:S(2)}, u32[]{:S(2)}) async-start(f32[16,1,800]{2,1,0:T(1,128)} %reshape.93), calls=%async_computation.3 | async-start | bytes 114688 | tf_op jit(solution)/shard_map/all_to_all | solution.py:93
  137.7 2.8 %copy-start.5 = (f32[2,25,64,128]{3,2,1,0:T(8,128)S(1)}, f32[2,25,64,128]{3,2,1,0:T(8,128)}, u32[]{:S(2)}) copy-start(f32[2,25,64,128]{3,2,1,0:T(8,128)} %get-tuple-element.15) | copy-start | bytes 4915204
  137.7 3.0 %copy-start.7 = (f32[2,25,64,129]{3,2,1,0:T(8,128)S(1)}, f32[2,25,64,129]{3,2,1,0:T(8,128)}, u32[]{:S(2)}) copy-start(f32[2,25,64,129]{3,2,1,0:T(8,128)} %add_multiply_fusion) | copy-start | bytes 4953604
  140.7 3.2 %copy-start.16 = (s32[64,128]{1,0:T(8,128)S(1)}, s32[64,128]{1,0:T(8,128)}, u32[]{:S(2)}) copy-start(s32[64,128]{1,0:T(8,128)} %param.13) | copy-start | bytes 98308
